TPU v7x, 512 devices: a whole 4x8x8 slice. The times are simulated.
512 devices in a mesh: tensor: 8 (over y), expert: 64 (over x, z, core).
Axes of the slice: x: 4, y: 8, z: 8, core: 2. Of those that a mesh axis runs over, the one named last changes fastest.
Arguments:
- attn_partial: bfloat16 [8, 4096, 4096], P('tensor', 'expert'), may hold values from -6 to 6
- norm_gain: float32 [4096], replicated, may hold values from 0.1 to 1.9
- expert_ids: int32 [4096, 8], P('expert'), may hold values from 0 to 63, all different within a row; in each aligned block of 8 rows (0 to 7, 8 to 15, ...) at most 2 rows name the same one
- route_weights: float32 [4096, 8], P('expert'), may hold values from 0.1 to 1
- gate_proj: bfloat16 [64, 4096, 1024], P('expert', None, 'tensor'), may hold values from -0.09375 to 0.09375
- up_proj: bfloat16 [64, 4096, 1024], P('expert', None, 'tensor'), may hold values from -0.09375 to 0.09375
- down_proj: bfloat16 [64, 1024, 4096], P('expert', None, 'tensor'), may hold values from -0.1875 to 0.1875
Outputs:
- combined: bfloat16 [4096, 4096], P(('expert', 'tensor'))
Inputs may be any that keep to these rules, and one draw needn't show every extreme that they name: `expert_ids`: each row names 8 different experts. In each aligned block of 8 rows (the rows of one device in the output's order) no expert is named by more than 2 rows, a bound that some block reaches.
All inputs are finite; a program needn't handle non-finite values.
Results may differ from a plain program's by a relative error of at most 0.025.
Values may be sent and summed in bfloat16 or wider, within the bound.
No kernel may reach another device: no remote copies, remote signals or barrier semaphores. Data moves between devices by JAX's collectives and lax.ppermute only.
A program may use at most 64 MiB of HBM per device.

v0:
```python
import jax
import jax.numpy as jnp
from jax import lax
from jax.sharding import PartitionSpec as P

QB = 128


def normalize_dequant(summed, norm_gain, block_width):
    row_count, feature_width = summed.shape
    mean_sq = jnp.mean(summed * summed, axis=-1, keepdims=True)
    normed = summed * lax.rsqrt(mean_sq + 1e-06) * norm_gain
    blocks = normed.reshape(row_count, feature_width // block_width, block_width)
    scales = ((jnp.max(jnp.abs(blocks), axis=-1) + 1e-06) / 448.0).astype(jnp.bfloat16)
    scale_f = scales.astype(jnp.float32)[:, :, None]
    values = (blocks / scale_f).astype(jnp.bfloat16)
    restored = (values.astype(jnp.float32) * scale_f).astype(jnp.bfloat16)
    return restored.reshape(row_count, feature_width)


def on_device(attn_partial, norm_gain, expert_ids, route_weights, gate_proj, up_proj, down_proj):
    tensor_count = lax.axis_size("tensor")
    expert_count = lax.axis_size("expert")
    tensor_index = lax.axis_index("tensor")
    group_tokens = expert_ids.shape[0]
    top_count = expert_ids.shape[1]
    row_count = group_tokens // tensor_count
    feature_width = attn_partial.shape[2]
    capacity = max(2, (2 * row_count * top_count + expert_count - 1) // expert_count)
    gate_matrix = gate_proj[0]
    up_matrix = up_proj[0]
    down_matrix = down_proj[0]
    column_share = down_matrix.shape[1]
    own_start = tensor_index * row_count
    own_ids = lax.dynamic_slice_in_dim(expert_ids, own_start, row_count, 0)
    own_weights = lax.dynamic_slice_in_dim(route_weights, own_start, row_count, 0)
    parts = lax.all_to_all(
        attn_partial[0].reshape(tensor_count, row_count, feature_width),
        "tensor",
        split_axis=0,
        concat_axis=0,
        tiled=True,
    )
    summed = jnp.sum(parts.astype(jnp.float32), axis=0)
    restored = normalize_dequant(summed, norm_gain, QB)
    labels = jnp.arange(expert_count, dtype=jnp.int32)
    hit = own_ids[..., None] == labels
    member = jnp.sum(hit.astype(jnp.int32), axis=1)
    earlier = jnp.cumsum(member, axis=0) - member
    places = jnp.arange(capacity, dtype=jnp.int32)
    chosen = (earlier[..., None] == places) & (member[..., None] > 0)
    send = jnp.einsum(
        "rec,rd->ecd", chosen.astype(jnp.bfloat16), restored, preferred_element_type=jnp.float32
    ).astype(jnp.bfloat16)
    recv = lax.all_to_all(send, "expert", split_axis=0, concat_axis=0, tiled=True)
    rows = lax.all_gather(recv, "tensor", axis=0, tiled=False)
    slot_total = tensor_count * expert_count * capacity
    rows = rows.reshape(slot_total, feature_width)
    gate_act = jnp.dot(rows, gate_matrix, preferred_element_type=jnp.float32)
    up_act = jnp.dot(rows, up_matrix, preferred_element_type=jnp.float32)
    hidden = (jax.nn.silu(gate_act) * up_act).astype(jnp.bfloat16)
    expert_sum = jnp.dot(
        lax.all_gather(hidden, "tensor", axis=1, tiled=True),
        down_matrix,
        preferred_element_type=jnp.float32,
    )
    expert_rows = expert_sum.astype(jnp.bfloat16).reshape(
        tensor_count, expert_count, capacity, column_share
    )
    returned = lax.all_to_all(
        lax.all_to_all(expert_rows, "tensor", split_axis=0, concat_axis=3, tiled=True),
        "expert",
        split_axis=1,
        concat_axis=1,
        tiled=True,
    )
    returned = returned.reshape(expert_count, capacity, feature_width)
    pair_weight = jnp.sum(jnp.where(hit, own_weights[..., None], 0.0), axis=1)
    mixing = jnp.where(chosen, pair_weight[..., None], 0.0)
    combined = jnp.einsum(
        "rec,ecd->rd", mixing, returned.astype(jnp.float32), precision=lax.Precision.HIGHEST
    )
    return combined.astype(jnp.bfloat16)


def solution(mesh):
    return jax.shard_map(
        on_device,
        mesh=mesh,
        in_specs=(
            P("tensor", "expert", None),
            P(),
            P("expert", None),
            P("expert", None),
            P("expert", None, "tensor"),
            P("expert", None, "tensor"),
            P("expert", None, "tensor"),
        ),
        out_specs=P(("expert", "tensor"), None),
        check_vma=False,
    )
```

profile of v0, /device:TPU:1, one launch (start us, length us, event | category | flops | bytes accessed | tf_op | source)
XLA Modules:
  0.0 320.2 jit_solution(14053400340128236630)
XLA Ops:
  6.5 0.0 copy-start
  6.5 7.8 %all-to-all-start = ((bf16[8,8,4096]{2,1,0:T(8,128)(2,1)}), bf16[8,8,4096]{2,1,0:T(8,128)(2,1)S(1)}, u32[]{:S(2)}, u32[]{:S(2)}) async-start(bf16[8,8,4096]{2,1,0:T(8,128)(2,1)} %bitcast.51), calls=%async_computation | async-start | bytes 1048576 | tf_op jit(solution)/shard_map/all_to_all | solution.py:37
  14.3 0.0 all-gather.6.cloned.1.call-start
  14.4 0.8 constant_dynamic-slice_fusion.1
  15.1 0.1 copy.36
  15.2 0.1 convert_reduce_fusion.1
  15.3 13.9 %all-to-all-done = bf16[8,8,4096]{2,1,0:T(8,128)(2,1)S(1)} async-done(((bf16[8,8,4096]{2,1,0:T(8,128)(2,1)}), bf16[8,8,4096]{2,1,0:T(8,128)(2,1)S(1)}, u32[]{:S(2)}, u32[]{:S(2)}) %all-to-all-start) | async-done | bytes 524320 | tf_op jit(solution)/shard_map/all_to_all | solution.py:37
  29.3 0.1 convert_reduce_fusion
  29.3 0.1 multiply_reduce_fusion
  29.5 0.9 fusion.12
  30.4 0.1 copy.38
  30.5 0.1 copy.39
  30.6 1.2 convolution_convert_fusion
  31.8 1.1 copy.40
  32.9 45.3 %all_to_all.33 = bf16[64,2,4096]{2,1,0:T(2,128)(2,1)} all-to-all(bf16[64,2,4096]{2,1,0:T(2,128)(2,1)S(1)} %copy.40), channel_id=1, replica_groups=mesh['tensor'=8,'expert'=64] {'expert'}, dimensions={0} | all-to-all | bytes 2097152 | tf_op jit(solution)/shard_map/all_to_all | solution.py:55
  78.1 0.0 all-gather.6.cloned.1.call-update
  78.2 0.0 copy-start.3
  78.2 0.0 all-gather.4.cloned.1.call-start
  78.2 87.9 %all-gather.6.cloned.1.call-done = bf16[512,2,4096]{2,1,0:T(2,128)(2,1)} async-done(((bf16[64,2,4096]{2,1,0:T(2,128)(2,1)}), bf16[512,2,4096]{2,1,0:T(2,128)(2,1)}) %all-gather.6.cloned.1.call-update) | async-done | bytes 8388624 | tf_op jit(solution)/shard_map/all_gather | solution.py:56
  166.1 13.1 %reshape.59 = bf16[1024,4096]{1,0:T(8,128)(2,1)} reshape(bf16[512,2,4096]{2,1,0:T(2,128)(2,1)} %all-gather.6.cloned.1.call-done) | data formatting | bytes 16777216 | tf_op jit(solution)/shard_map/reshape | solution.py:58
  179.2 0.0 copy-done.3
  179.2 0.0 copy-start.1
  179.2 0.0 copy-start.4
  179.2 5.9 %fusion.5 = f32[1024,128]{1,0:T(8,128)S(1)} fusion(bf16[1024,4096]{1,0:T(8,128)(2,1)} %reshape.59, bf16[1,4096,128]{2,1,0:T(8,128)(2,1)S(1)} %copy-done.3), kind=kOutput, calls=%fused_computation.9 | convolution fusion | flops 1073741824 | bytes 9961472 | tf_op jit(solution)/shard_map/dot_general | solution.py:59
  185.1 0.0 copy-done.1
  185.1 0.1 copy-done.4
  185.2 3.1 fusion.1
  188.3 0.0 all-gather.4.cloned.1.call-update
  188.3 0.0 copy-start.2
  188.3 44.5 %all-gather.4.cloned.1.call-done = bf16[1024,1024]{1,0:T(8,128)(2,1)} async-done(((bf16[1024,128]{1,0:T(8,128)(2,1)}), bf16[1024,1024]{1,0:T(8,128)(2,1)}) %all-gather.4.cloned.1.call-update) | async-done | bytes 2097168 | tf_op jit(solution)/shard_map/all_gather | solution.py:63
  232.8 0.0 copy-done
  232.8 2.8 convolution_convert_fusion.1
  235.7 0.4 reshape.60
  236.1 25.8 %all_to_all.34 = bf16[8,64,2,512]{3,2,1,0:T(2,128)(2,1)S(1)} all-to-all(bf16[8,64,2,512]{3,2,1,0:T(2,128)(2,1)S(1)} %reshape.60), channel_id=1, replica_groups=mesh['tensor'=8,'expert'=64] {'tensor'}, dimensions={0} | all-to-all | bytes 2097152 | tf_op jit(solution)/shard_map/all_to_all | solution.py:71
  261.9 1.1 copy.41
  263.0 1.6 all_to_all.27
  264.6 18.1 %all-to-all-start.3 = ((bf16[1,64,2,4096]{3,2,0,1:T(2,128)(2,1)}), bf16[1,64,2,4096]{3,2,0,1:T(2,128)(2,1)S(1)}, u32[]{:S(2)}, u32[]{:S(2)}) async-start(bf16[1,64,2,4096]{3,2,0,1:T(2,128)(2,1)} %all_to_all.27), calls=%async_computation.3 | async-start | bytes 2097152 | tf_op jit(solution)/shard_map/all_to_all | solution.py:70
  282.7 0.0 copy-done.2
  282.7 0.1 constant_dynamic-slice_fusion
  282.8 0.1 copy.37
  282.9 0.1 select_reduce_fusion
  282.9 28.3 %all-to-all-done.3 = bf16[1,64,2,4096]{3,2,0,1:T(2,128)(2,1)S(1)} async-done(((bf16[1,64,2,4096]{3,2,0,1:T(2,128)(2,1)}), bf16[1,64,2,4096]{3,2,0,1:T(2,128)(2,1)S(1)}, u32[]{:S(2)}, u32[]{:S(2)}) %all-to-all-start.3) | async-done | bytes 1048608 | tf_op jit(solution)/shard_map/all_to_all | solution.py:70
  311.2 2.2 fusion
  (5 shorter events, 0.1 us)
Async XLA Ops:
  6.5 226.3 %copy-start = (bf16[1,1024,512]{2,1,0:T(8,128)(2,1)S(1)}, bf16[1,1024,512]{2,1,0:T(8,128)(2,1)}, u32[]{:S(2)}) copy-start(bf16[1,1024,512]{2,1,0:T(8,128)(2,1)} %param.13) | copy-start | bytes 3145732
  6.5 22.7 %all-to-all-start = ((bf16[8,8,4096]{2,1,0:T(8,128)(2,1)}), bf16[8,8,4096]{2,1,0:T(8,128)(2,1)S(1)}, u32[]{:S(2)}, u32[]{:S(2)}) async-start(bf16[8,8,4096]{2,1,0:T(8,128)(2,1)} %bitcast.51), calls=%async_computation | async-start | bytes 1048576 | tf_op jit(solution)/shard_map/all_to_all | solution.py:37
  14.3 151.8 %all-gather.6.cloned.1.call-start = ((), (), s32[]{:S(2)}) async-start(), calls=%async_computation.5 | async-start | bytes 9437184 | tf_op jit(solution)/shard_map/all_gather | solution.py:56
  78.2 101.1 %copy-start.3 = (bf16[1,4096,128]{2,1,0:T(8,128)(2,1)S(1)}, bf16[1,4096,128]{2,1,0:T(8,128)(2,1)}, u32[]{:S(2)}) copy-start(bf16[1,4096,128]{2,1,0:T(8,128)(2,1)} %param.11) | copy-start | bytes 3145732
  78.2 154.6 %all-gather.4.cloned.1.call-start = ((), (), s32[]{:S(2)}) async-start(), calls=%async_computation.4 | async-start | bytes 2359296 | tf_op jit(solution)/shard_map/all_gather | solution.py:63
  179.2 5.9 %copy-start.1 = (bf16[1024,4096]{1,0:T(8,128)(2,1)S(1)}, bf16[1024,4096]{1,0:T(8,128)(2,1)}, u32[]{:S(2)}) copy-start(bf16[1024,4096]{1,0:T(8,128)(2,1)} %reshape.59) | copy-start | bytes 25165828
  179.2 6.0 %copy-start.4 = (bf16[1,4096,128]{2,1,0:T(8,128)(2,1)S(1)}, bf16[1,4096,128]{2,1,0:T(8,128)(2,1)}, u32[]{:S(2)}) copy-start(bf16[1,4096,128]{2,1,0:T(8,128)(2,1)} %param.12) | copy-start | bytes 3145732
  188.3 94.4 %copy-start.2 = (f32[64,8]{0,1:T(8,128)S(1)}, f32[64,8]{0,1:T(8,128)}, u32[]{:S(2)}) copy-start(f32[64,8]{0,1:T(8,128)} %param.10) | copy-start | bytes 6148
  264.6 46.6 %all-to-all-start.3 = ((bf16[1,64,2,4096]{3,2,0,1:T(2,128)(2,1)}), bf16[1,64,2,4096]{3,2,0,1:T(2,128)(2,1)S(1)}, u32[]{:S(2)}, u32[]{:S(2)}) async-start(bf16[1,64,2,4096]{3,2,0,1:T(2,128)(2,1)} %all_to_all.27), calls=%async_computation.3 | async-start | bytes 2097152 | tf_op jit(solution)/shard_map/all_to_all | solution.py:70
Sparse Core Ops, SparseCore 0:
  78.3 87.8 all-gather.5
  188.4 44.3 all-gather.3
where the time goes:
time: 321 us; the launch traced here: 320 us
  waiting for transfers between devices  175 us (55%)
  blocking collectives  71 us (22%)
  starting transfers between devices  25.9 us (8%)
  local copies, waits for them, and re-layouts  18.6 us (6%)
  matrix products  15.1 us (5%)
  between operations  13.5 us (4%)
    all_gather x1, waiting for transfers between devices, on_device(): rows = lax.all_gather(recv, 'tensor', axis=0, tiled=False)  87.9 us
    all_to_all x1, blocking collectives, on_device(): lax.all_to_all(send, 'expert', split_axis=0, concat_axis=0, tiled=True)  45.3 us
    all_gather x1, waiting for transfers between devices, on_device(): lax.all_gather(hidden, 'tensor', axis=1, tiled=True)  44.5 us
    all_to_all x1, waiting for transfers between devices, on_device(): lax.all_to_all(lax.all_to_all(expert_rows, 'tensor', split_axis=0, concat...  28.3 us
    all_to_all x1, blocking collectives, on_device(): lax.all_to_all(expert_rows, 'tensor', split_axis=0, concat_axis=3, tiled=...  25.8 us
    all_to_all x1, starting transfers between devices, on_device(): lax.all_to_all(lax.all_to_all(expert_rows, 'tensor', split_axis=0, concat...  18.1 us
    all_to_all x1, waiting for transfers between devices, on_device(): lax.all_to_all(attn_partial[0].reshape(tensor_count, row_count, feature_w...  13.9 us
    reshape x1, local copies, waits for them, and re-layouts, on_device(): rows = rows.reshape(slot_total, feature_width)  13.1 us
  transfers between devices with their start and end apart: 4, of which 4 were waited for; matrix products, arithmetic and copies ran while one was open for 0% of the time, Pallas kernels for 0%

commit v1 on v0

--- a/solution.py
+++ b/solution.py
@@ -4,6 +4,22 @@
 from jax.sharding import PartitionSpec as P
 
 QB = 128
+
+
+def collect(x, axis, dim):
+    ways, here, turn = (lax.axis_size(axis), lax.axis_index(axis), x.shape[dim])
+    lengths = [n * ways if d == dim else n for d, n in enumerate(x.shape)]
+    full = lax.dynamic_update_slice_in_dim(jnp.zeros(lengths, x.dtype), x, here * turn, axis=dim)
+    going_up = going_down = x
+    for far in range(1, ways // 2 + 1):
+        going_up = lax.ppermute(going_up, axis, [(d, (d + 1) % ways) for d in range(ways)])
+        full = lax.dynamic_update_slice_in_dim(full, going_up, (here - far) % ways * turn, axis=dim)
+        if 2 * far < ways:
+            going_down = lax.ppermute(going_down, axis, [(d, (d - 1) % ways) for d in range(ways)])
+            full = lax.dynamic_update_slice_in_dim(
+                full, going_down, (here + far) % ways * turn, axis=dim
+            )
+    return full
 
 
 def normalize_dequant(summed, norm_gain, block_width):
@@ -60,9 +76,7 @@
     up_act = jnp.dot(rows, up_matrix, preferred_element_type=jnp.float32)
     hidden = (jax.nn.silu(gate_act) * up_act).astype(jnp.bfloat16)
     expert_sum = jnp.dot(
-        lax.all_gather(hidden, "tensor", axis=1, tiled=True),
-        down_matrix,
-        preferred_element_type=jnp.float32,
+        collect(hidden, "tensor", 1), down_matrix, preferred_element_type=jnp.float32
     )
     expert_rows = expert_sum.astype(jnp.bfloat16).reshape(
         tensor_count, expert_count, capacity, column_share

time: 321 us -> 314 us (0.978)
  waiting for transfers between devices: 175 us -> 143 us
  starting transfers between devices: 25.9 us -> 45.7 us
  local copies, waits for them, and re-layouts: 18.6 us -> 23.2 us
    all_gather x1 -> x0, waiting for transfers between devices: 44.5 us -> none  [on_device(): lax.all_gather(hidden, 'tensor', axis=1, tiled=True)]
    ppermute x0 -> x7, starting transfers between devices: none -> 21.4 us  [the longest x3 13.7 us: collect(): lax.ppermute(going_down, axis, [(d, (d - 1) % ways) for d in range(ways)])]
    ppermute x0 -> x7, waiting for transfers between devices: none -> 12.8 us  [the longest x4 12.7 us: collect(): lax.ppermute(going_up, axis, [(d, (d + 1) % ways) for d in range(ways)])]
    dynamic_update_slice x0 -> x7, local copies, waits for them, and re-layouts: none -> 3.46 us  [the longest x4 2.25 us: collect(): lax.dynamic_update_slice_in_dim(full, going_up, (here - far) % ways * tur...]
  transfers between devices with their start and end apart: 4 -> 10, of which waited for: 4 -> 7; matrix products, arithmetic and copies ran while one was open for 0% -> 1% of each run, Pallas kernels for 0% -> 0%
where the time goes in v1:
time: 314 us; the launch traced here: 313 us
  waiting for transfers between devices  143 us (46%)
  blocking collectives  72.8 us (23%)
  starting transfers between devices  45.7 us (15%)
  local copies, waits for them, and re-layouts  23.2 us (7%)
  between operations  13.8 us (4%)
  matrix products  13.2 us (4%)
    all_gather x1, waiting for transfers between devices, on_device(): rows = lax.all_gather(recv, 'tensor', axis=0, tiled=False)  88 us
    all_to_all x1, blocking collectives, on_device(): lax.all_to_all(send, 'expert', split_axis=0, concat_axis=0, tiled=True)  45.3 us
    all_to_all x1, waiting for transfers between devices, on_device(): lax.all_to_all(lax.all_to_all(expert_rows, 'tensor', split_axis=0, concat...  28.3 us
    all_to_all x1, blocking collectives, on_device(): lax.all_to_all(expert_rows, 'tensor', split_axis=0, concat_axis=3, tiled=...  27.5 us
    all_to_all x1, starting transfers between devices, on_device(): lax.all_to_all(lax.all_to_all(expert_rows, 'tensor', split_axis=0, concat...  16.5 us
    all_to_all x1, waiting for transfers between devices, on_device(): lax.all_to_all(attn_partial[0].reshape(tensor_count, row_count, feature_w...  13.9 us
    ppermute x3, starting transfers between devices, collect(): lax.ppermute(going_down, axis, [(d, (d - 1) % ways) for d in range(ways)])  13.7 us
    reshape x1, local copies, waits for them, and re-layouts, on_device(): rows = rows.reshape(slot_total, feature_width)  13.1 us
  transfers between devices with their start and end apart: 10, of which 7 were waited for; matrix products, arithmetic and copies ran while one was open for 1% of the time, Pallas kernels for 0%

profile of v1, /device:TPU:1, one launch (start us, length us, event | category | flops | bytes accessed | tf_op | source)
XLA Modules:
  0.0 313.0 jit_solution(572868152509308433)
XLA Ops:
  6.5 0.0 copy-start
  6.5 0.0 copy-start.2
  6.5 7.8 %all-to-all-start = ((bf16[8,8,4096]{2,1,0:T(8,128)(2,1)}), bf16[8,8,4096]{2,1,0:T(8,128)(2,1)S(1)}, u32[]{:S(2)}, u32[]{:S(2)}) async-start(bf16[8,8,4096]{2,1,0:T(8,128)(2,1)} %bitcast.53), calls=%async_computation | async-start | bytes 1048576 | tf_op jit(solution)/shard_map/all_to_all | solution.py:53
  14.3 0.0 all-gather.3.cloned.1.call-start
  14.4 0.8 constant_dynamic-slice_fusion.1
  15.1 0.1 copy.36
  15.2 0.1 convert_reduce_fusion.1
  15.3 13.9 %all-to-all-done = bf16[8,8,4096]{2,1,0:T(8,128)(2,1)S(1)} async-done(((bf16[8,8,4096]{2,1,0:T(8,128)(2,1)}), bf16[8,8,4096]{2,1,0:T(8,128)(2,1)S(1)}, u32[]{:S(2)}, u32[]{:S(2)}) %all-to-all-start) | async-done | bytes 524320 | tf_op jit(solution)/shard_map/all_to_all | solution.py:53
  29.3 0.1 convert_reduce_fusion
  29.3 0.1 multiply_reduce_fusion
  29.5 0.9 fusion.12
  30.4 0.1 copy.38
  30.5 0.1 copy.39
  30.6 0.0 copy-done.2
  30.6 0.5 convolution_convert_fusion
  31.1 1.1 copy.40
  32.2 45.3 %all_to_all.33 = bf16[64,2,4096]{2,1,0:T(2,128)(2,1)} all-to-all(bf16[64,2,4096]{2,1,0:T(2,128)(2,1)S(1)} %copy.40), channel_id=1, replica_groups=mesh['tensor'=8,'expert'=64] {'expert'}, dimensions={0} | all-to-all | bytes 2097152 | tf_op jit(solution)/shard_map/all_to_all | solution.py:71
  77.4 0.0 all-gather.3.cloned.1.call-update
  77.5 0.0 copy-start.4
  77.5 88.0 %all-gather.3.cloned.1.call-done = bf16[512,2,4096]{2,1,0:T(2,128)(2,1)} async-done(((bf16[64,2,4096]{2,1,0:T(2,128)(2,1)}), bf16[512,2,4096]{2,1,0:T(2,128)(2,1)}) %all-gather.3.cloned.1.call-update) | async-done | bytes 8388624 | tf_op jit(solution)/shard_map/all_gather | solution.py:72
  165.4 13.1 %reshape.59 = bf16[1024,4096]{1,0:T(8,128)(2,1)} reshape(bf16[512,2,4096]{2,1,0:T(2,128)(2,1)} %all-gather.3.cloned.1.call-done) | data formatting | bytes 16777216 | tf_op jit(solution)/shard_map/reshape | solution.py:74
  178.5 0.0 copy-done.4
  178.5 0.0 copy-start.1
  178.5 5.9 %fusion.5 = f32[1024,128]{1,0:T(8,128)S(1)} fusion(bf16[1024,4096]{1,0:T(8,128)(2,1)} %reshape.59, bf16[1,4096,128]{2,1,0:T(8,128)(2,1)S(1)} %copy-done.4), kind=kOutput, calls=%fused_computation.9 | convolution fusion | flops 1073741824 | bytes 9961472 | tf_op jit(solution)/shard_map/dot_general | solution.py:75
  184.4 0.3 broadcast_in_dim.41
  184.7 0.0 copy-done
  184.7 0.0 copy-done.1
  184.7 2.4 constant_dynamic-update-slice_fusion.7
  187.1 1.9 collective-permute-start
  189.0 4.6 %collective-permute-start.1 = (bf16[1024,128]{1,0:T(8,128)(2,1)S(1)}, bf16[1024,128]{1,0:T(8,128)(2,1)}, u32[]{:S(2)}, u32[]{:S(2)}) collective-permute-start(bf16[1024,128]{1,0:T(8,128)(2,1)S(1)} %get-tuple-element.6), channel_id=1, source_target_pairs={{0,448},{64,0},{128,64},{192,128},{256,192},{320,256},{384,320},{4... | collective-permute-start | bytes 786440 | tf_op jit(solution)/shard_map/ppermute | solution.py:18
  193.6 3.7 %collective-permute-done = bf16[1024,128]{1,0:T(8,128)(2,1)} collective-permute-done((bf16[1024,128]{1,0:T(8,128)(2,1)S(1)}, bf16[1024,128]{1,0:T(8,128)(2,1)}, u32[]{:S(2)}, u32[]{:S(2)}) %collective-permute-start) | collective-permute-done | bytes 262176 | tf_op jit(solution)/shard_map/ppermute | solution.py:15
  197.4 1.9 collective-permute-start.2
  199.3 0.0 collective-permute-done.1
  199.3 4.6 %collective-permute-start.3 = (bf16[1024,128]{1,0:T(8,128)(2,1)}, bf16[1024,128]{1,0:T(8,128)(2,1)S(1)}, u32[]{:S(2)}, u32[]{:S(2)}) collective-permute-start(bf16[1024,128]{1,0:T(8,128)(2,1)} %collective-permute-done.1), channel_id=1, source_target_pairs={{0,448},{64,0},{128,64},{192,128},{256,192},{320,256},{384,320},{4... | collective-permute-start | bytes 786440 | tf_op jit(solution)/shard_map/ppermute | solution.py:18
  204.0 0.0 copy-start.5
  204.0 2.9 collective-permute-done.2
  206.9 1.9 collective-permute-start.4
  208.9 1.0 constant_dynamic-update-slice_fusion.6
  209.9 1.0 constant_dynamic-update-slice_fusion.5
  210.9 0.0 collective-permute-done.3
  211.0 4.6 %collective-permute-start.5 = (bf16[1024,128]{1,0:T(8,128)(2,1)S(1)}, bf16[1024,128]{1,0:T(8,128)(2,1)S(1)}, u32[]{:S(2)}, u32[]{:S(2)}) collective-permute-start(bf16[1024,128]{1,0:T(8,128)(2,1)S(1)} %collective-permute-done.3), channel_id=1, source_target_pairs={{0,448},{64,0},{128,64},{192,128},{256,192},{320,256},{384,320},{4... | collective-permute-start | bytes 786440 | tf_op jit(solution)/shard_map/ppermute | solution.py:18
  215.5 1.0 constant_dynamic-update-slice_fusion.4
  216.6 0.0 collective-permute-done.4
  216.6 1.9 collective-permute-start.6
  218.5 0.1 constant_dynamic-update-slice_fusion.3
  218.6 0.1 constant_dynamic-update-slice_fusion.2
  218.7 0.1 collective-permute-done.5
  218.8 0.1 constant_dynamic-update-slice_fusion.1
  218.9 6.0 %collective-permute-done.6 = bf16[1024,128]{1,0:T(8,128)(2,1)S(1)} collective-permute-done((bf16[1024,128]{1,0:T(8,128)(2,1)S(1)}, bf16[1024,128]{1,0:T(8,128)(2,1)S(1)}, u32[]{:S(2)}, u32[]{:S(2)}) %collective-permute-start.6) | collective-permute-done | bytes 262176 | tf_op jit(solution)/shard_map/ppermute | solution.py:15
  224.9 0.1 constant_dynamic-update-slice_fusion
  225.0 0.0 copy-done.5
  225.0 2.2 convolution_convert_fusion.1
  227.2 1.5 reshape.60
  228.7 27.5 %all_to_all.34 = bf16[8,64,2,512]{3,2,1,0:T(2,128)(2,1)S(1)} all-to-all(bf16[8,64,2,512]{3,2,1,0:T(2,128)(2,1)S(1)} %reshape.60), channel_id=1, replica_groups=mesh['tensor'=8,'expert'=64] {'tensor'}, dimensions={0} | all-to-all | bytes 2097152 | tf_op jit(solution)/shard_map/all_to_all | solution.py:85
  256.2 1.1 copy.41
  257.4 0.0 copy-start.3
  257.4 1.6 all_to_all.27
  258.9 16.5 %all-to-all-start.3 = ((bf16[1,64,2,4096]{3,2,0,1:T(2,128)(2,1)}), bf16[1,64,2,4096]{3,2,0,1:T(2,128)(2,1)S(1)}, u32[]{:S(2)}, u32[]{:S(2)}) async-start(bf16[1,64,2,4096]{3,2,0,1:T(2,128)(2,1)} %all_to_all.27), calls=%async_computation.3 | async-start | bytes 2097152 | tf_op jit(solution)/shard_map/all_to_all | solution.py:84
  275.4 0.0 copy-done.3
  275.4 0.1 constant_dynamic-slice_fusion
  275.5 0.1 copy.37
  275.6 0.1 select_reduce_fusion
  275.7 28.3 %all-to-all-done.3 = bf16[1,64,2,4096]{3,2,0,1:T(2,128)(2,1)S(1)} async-done(((bf16[1,64,2,4096]{3,2,0,1:T(2,128)(2,1)}), bf16[1,64,2,4096]{3,2,0,1:T(2,128)(2,1)S(1)}, u32[]{:S(2)}, u32[]{:S(2)}) %all-to-all-start.3) | async-done | bytes 1048608 | tf_op jit(solution)/shard_map/all_to_all | solution.py:84
  304.0 2.2 fusion
  (5 shorter events, 0.1 us)
Async XLA Ops:
  6.5 178.1 %copy-start = (bf16[1,4096,128]{2,1,0:T(8,128)(2,1)S(1)}, bf16[1,4096,128]{2,1,0:T(8,128)(2,1)}, u32[]{:S(2)}) copy-start(bf16[1,4096,128]{2,1,0:T(8,128)(2,1)} %param.12) | copy-start | bytes 3145732
  6.5 24.0 %copy-start.2 = (f32[4096]{0:T(1024)S(1)}, f32[4096]{0:T(1024)}, u32[]{:S(2)}) copy-start(f32[4096]{0:T(1024)} %param.8) | copy-start | bytes 49156
  6.5 22.7 %all-to-all-start = ((bf16[8,8,4096]{2,1,0:T(8,128)(2,1)}), bf16[8,8,4096]{2,1,0:T(8,128)(2,1)S(1)}, u32[]{:S(2)}, u32[]{:S(2)}) async-start(bf16[8,8,4096]{2,1,0:T(8,128)(2,1)} %bitcast.53), calls=%async_computation | async-start | bytes 1048576 | tf_op jit(solution)/shard_map/all_to_all | solution.py:53
  14.3 151.1 %all-gather.3.cloned.1.call-start = ((), (), s32[]{:S(2)}) async-start(), calls=%async_computation.4 | async-start | bytes 9437184 | tf_op jit(solution)/shard_map/all_gather | solution.py:72
  77.5 101.1 %copy-start.4 = (bf16[1,4096,128]{2,1,0:T(8,128)(2,1)S(1)}, bf16[1,4096,128]{2,1,0:T(8,128)(2,1)}, u32[]{:S(2)}) copy-start(bf16[1,4096,128]{2,1,0:T(8,128)(2,1)} %param.11) | copy-start | bytes 3145732
  178.5 6.1 %copy-start.1 = (bf16[1024,4096]{1,0:T(8,128)(2,1)S(1)}, bf16[1024,4096]{1,0:T(8,128)(2,1)}, u32[]{:S(2)}) copy-start(bf16[1024,4096]{1,0:T(8,128)(2,1)} %reshape.59) | copy-start | bytes 25165828
  187.1 10.2 %collective-permute-start = (bf16[1024,128]{1,0:T(8,128)(2,1)S(1)}, bf16[1024,128]{1,0:T(8,128)(2,1)}, u32[]{:S(2)}, u32[]{:S(2)}) collective-permute-start(bf16[1024,128]{1,0:T(8,128)(2,1)S(1)} %get-tuple-element.6), channel_id=1, source_target_pairs={{0,64},{64,128},{128,192},{192,256},{256,320},{320,384},{384,448},... | collective-permute-start | bytes 786440 | tf_op jit(solution)/shard_map/ppermute | solution.py:15
  189.0 10.2 %collective-permute-start.1 = (bf16[1024,128]{1,0:T(8,128)(2,1)S(1)}, bf16[1024,128]{1,0:T(8,128)(2,1)}, u32[]{:S(2)}, u32[]{:S(2)}) collective-permute-start(bf16[1024,128]{1,0:T(8,128)(2,1)S(1)} %get-tuple-element.6), channel_id=1, source_target_pairs={{0,448},{64,0},{128,64},{192,128},{256,192},{320,256},{384,320},{4... | collective-permute-start | bytes 786440 | tf_op jit(solution)/shard_map/ppermute | solution.py:18
  197.4 9.6 %collective-permute-start.2 = (bf16[1024,128]{1,0:T(8,128)(2,1)}, bf16[1024,128]{1,0:T(8,128)(2,1)}, u32[]{:S(2)}, u32[]{:S(2)}) collective-permute-start(bf16[1024,128]{1,0:T(8,128)(2,1)} %collective-permute-done), channel_id=1, source_target_pairs={{0,64},{64,128},{128,192},{192,256},{256,320},{320,384},{384,448},... | collective-permute-start | bytes 786440 | tf_op jit(solution)/shard_map/ppermute | solution.py:15
  199.3 11.7 %collective-permute-start.3 = (bf16[1024,128]{1,0:T(8,128)(2,1)}, bf16[1024,128]{1,0:T(8,128)(2,1)S(1)}, u32[]{:S(2)}, u32[]{:S(2)}) collective-permute-start(bf16[1024,128]{1,0:T(8,128)(2,1)} %collective-permute-done.1), channel_id=1, source_target_pairs={{0,448},{64,0},{128,64},{192,128},{256,192},{320,256},{384,320},{4... | collective-permute-start | bytes 786440 | tf_op jit(solution)/shard_map/ppermute | solution.py:18
  204.0 21.0 %copy-start.5 = (bf16[1,1024,512]{2,1,0:T(8,128)(2,1)S(1)}, bf16[1,1024,512]{2,1,0:T(8,128)(2,1)}, u32[]{:S(2)}) copy-start(bf16[1,1024,512]{2,1,0:T(8,128)(2,1)} %param.13) | copy-start | bytes 3145732
  206.9 9.6 %collective-permute-start.4 = (bf16[1024,128]{1,0:T(8,128)(2,1)}, bf16[1024,128]{1,0:T(8,128)(2,1)S(1)}, u32[]{:S(2)}, u32[]{:S(2)}) collective-permute-start(bf16[1024,128]{1,0:T(8,128)(2,1)} %collective-permute-done.2), channel_id=1, source_target_pairs={{0,64},{64,128},{128,192},{192,256},{256,320},{320,384},{384,448},... | collective-permute-start | bytes 786440 | tf_op jit(solution)/shard_map/ppermute | solution.py:15
  211.0 7.9 %collective-permute-start.5 = (bf16[1024,128]{1,0:T(8,128)(2,1)S(1)}, bf16[1024,128]{1,0:T(8,128)(2,1)S(1)}, u32[]{:S(2)}, u32[]{:S(2)}) collective-permute-start(bf16[1024,128]{1,0:T(8,128)(2,1)S(1)} %collective-permute-done.3), channel_id=1, source_target_pairs={{0,448},{64,0},{128,64},{192,128},{256,192},{320,256},{384,320},{4... | collective-permute-start | bytes 786440 | tf_op jit(solution)/shard_map/ppermute | solution.py:18
  216.6 8.3 %collective-permute-start.6 = (bf16[1024,128]{1,0:T(8,128)(2,1)S(1)}, bf16[1024,128]{1,0:T(8,128)(2,1)S(1)}, u32[]{:S(2)}, u32[]{:S(2)}) collective-permute-start(bf16[1024,128]{1,0:T(8,128)(2,1)S(1)} %collective-permute-done.4), channel_id=1, source_target_pairs={{0,64},{64,128},{128,192},{192,256},{256,320},{320,384},{384,448},... | collective-permute-start | bytes 786440 | tf_op jit(solution)/shard_map/ppermute | solution.py:15
  257.4 18.1 %copy-start.3 = (f32[64,8]{0,1:T(8,128)S(1)}, f32[64,8]{0,1:T(8,128)}, u32[]{:S(2)}) copy-start(f32[64,8]{0,1:T(8,128)} %param.10) | copy-start | bytes 6148
  258.9 45.0 %all-to-all-start.3 = ((bf16[1,64,2,4096]{3,2,0,1:T(2,128)(2,1)}), bf16[1,64,2,4096]{3,2,0,1:T(2,128)(2,1)S(1)}, u32[]{:S(2)}, u32[]{:S(2)}) async-start(bf16[1,64,2,4096]{3,2,0,1:T(2,128)(2,1)} %all_to_all.27), calls=%async_computation.3 | async-start | bytes 2097152 | tf_op jit(solution)/shard_map/all_to_all | solution.py:84
Sparse Core Ops, SparseCore 0:
  77.6 87.8 all-gather.2
